TPU v7x, 256 devices: a whole 4x4x8 slice. The times are simulated.
256 devices in a mesh: cfg: 2 (over z_lo), seq: 16 (over z_hi, x), wblk: 8 (over y, core).
Axes of the slice: x: 4, y: 4, z: 8 (z_hi: 4, z_lo: 2; z = z_hi * 2 + z_lo), core: 2. Of those that a mesh axis runs over, the one named last changes fastest.
Arguments:
- text_tokens: bfloat16 [2, 2, 512, 3072], P('cfg', None, 'seq', 'wblk'), may hold values from -16 to 16
- image_tokens: bfloat16 [2, 4096, 3072], P(None, 'seq', 'wblk'), may hold values from -16 to 16
- pooled_vector: float32 [2, 3072], P('cfg', 'seq'), may hold values from -6 to 6
- mod_weight: bfloat16 [3072, 3, 3072], P('seq', None, 'wblk'), may hold values from -0.109375 to 0.109375
- qkv_weight: bfloat16 [3072, 3, 16, 128], P('seq', None, 'wblk'), may hold values from -0.109375 to 0.109375
- up_weight: bfloat16 [3072, 6144], P('seq', 'wblk'), may hold values from -0.109375 to 0.109375
- query_gain: float32 [128], replicated, may hold values from 0.6 to 10
- key_gain: float32 [128], replicated, may hold values from 0.6 to 10
- attn_weight: bfloat16 [2048, 3072], P('wblk', 'seq'), may hold values from -0.125 to 0.125
- down_weight: bfloat16 [6144, 3072], P('wblk', 'seq'), may hold values from -0.078125 to 0.078125
- lengths: int32 [2], replicated, may hold values from 1 to 512, as said below
- timestep: int32 [1], replicated, may hold values from 0 to 27
Outputs:
- text_out: bfloat16 [2, 2, 512, 3072], P('cfg', None, 'seq', 'wblk')
- velocity: float32 [2, 4096, 3072], P('cfg', 'seq', 'wblk')
- new_image: float32 [2, 4096, 3072], P('cfg', 'seq', 'wblk')
Inputs may be any that keep to these rules, and one draw needn't show every extreme that they name: `lengths`: some prompt has all 512 text tokens live in every draw.
All inputs are finite; a program needn't handle non-finite values.
Results may differ from a plain program's by a relative error of at most 0.025.
Values may be sent and summed in bfloat16 or wider, within the bound.
No kernel may reach another device: no remote copies, remote signals or barrier semaphores. Data moves between devices by JAX's collectives and lax.ppermute only.
A program may use at most 128 MiB of HBM per device.

v0:
```python
import math
import jax
import jax.numpy as jnp
from jax import lax
from jax.sharding import PartitionSpec as P

D = 3072
HD = 128
GRID = 64
STEPS = 28
epsilon = 1e-06
guidance = 3.5
time_shift = 3.0
rope_theta = 10000.0


def plan(timestep):
    step_index = timestep[0].astype(jnp.float32)
    time_now = 1.0 - step_index / STEPS
    time_next = 1.0 - (step_index + 1.0) / STEPS
    sigma_now = time_shift * time_now / (1.0 + (time_shift - 1.0) * time_now)
    sigma_next = time_shift * time_next / (1.0 + (time_shift - 1.0) * time_next)
    return (sigma_now, sigma_next - sigma_now)


def time_embedding(sigma_now, dim_count):
    halfwidth = dim_count // 2
    frequency = jnp.exp(-math.log(10000.0) * jnp.arange(halfwidth, dtype=jnp.float32) / halfwidth)
    angles = 1000.0 * sigma_now * frequency
    return jnp.concatenate([jnp.cos(angles), jnp.sin(angles)])


def inverse_freq(dim_count):
    return rope_theta ** (-jnp.arange(0, dim_count, 2, dtype=jnp.float32) / dim_count)


def rotary_angles(height_pos, width_pos):
    still_dims = HD // 8
    axis_dims = (HD - still_dims) // 2
    return jnp.concatenate(
        [
            jnp.zeros((height_pos.shape[0], still_dims // 2), jnp.float32),
            height_pos[:, None] * inverse_freq(axis_dims)[None],
            width_pos[:, None] * inverse_freq(axis_dims)[None],
        ],
        axis=1,
    )


def rotate(vectors, angles):
    paired_dims = vectors.reshape(vectors.shape[:-1] + (HD // 2, 2))
    cosine_table = jnp.cos(angles)[:, None, :]
    sine_table = jnp.sin(angles)[:, None, :]
    first_part = paired_dims[..., 0]
    second_part = paired_dims[..., 1]
    turned = jnp.stack(
        [
            first_part * cosine_table - second_part * sine_table,
            first_part * sine_table + second_part * cosine_table,
        ],
        axis=-1,
    )
    return turned.reshape(vectors.shape)


def head_norm(vectors, gain_vector):
    return (
        vectors
        * lax.rsqrt(jnp.mean(vectors * vectors, axis=-1, keepdims=True) + epsilon)
        * gain_vector
    )


def input_folder(source, pieces):
    width_rows = pieces[0].shape[0]
    first_total = jnp.dot(
        source, pieces[0].reshape(width_rows, -1), preferred_element_type=jnp.float32
    )
    second_total = jnp.dot(source, pieces[1], preferred_element_type=jnp.float32)
    return (first_total, second_total)


def output_folder(attended, activated, pieces):
    block_cols = jnp.dot(attended, pieces[0], preferred_element_type=jnp.float32)
    block_cols = block_cols + jnp.dot(activated, pieces[1], preferred_element_type=jnp.float32)
    return block_cols


def shards(
    text_tokens,
    image_tokens,
    pooled_vector,
    mod_weight,
    qkv_weight,
    up_weight,
    query_gain,
    key_gain,
    attn_weight,
    down_weight,
    lengths,
    timestep,
):
    seq_pos = lax.axis_index("seq")
    cfg_pos = lax.axis_index("cfg")
    prompts = image_tokens.shape[0]
    image_rows = image_tokens.shape[1]
    text_rows = text_tokens.shape[2]
    local_len = text_rows + image_rows
    dim_local = image_tokens.shape[2]
    dim_seq = pooled_vector.shape[1]
    heads_local = qkv_weight.shape[2]
    row_count = prompts * local_len
    sigma_now, step_size = plan(timestep)
    embedded = lax.dynamic_slice_in_dim(time_embedding(sigma_now, D), seq_pos * dim_seq, dim_seq)
    cond_vec = jax.nn.silu(pooled_vector[0] + embedded).astype(jnp.bfloat16)[None]
    mod_terms = jnp.dot(
        cond_vec, mod_weight.reshape(dim_seq, 3 * dim_local), preferred_element_type=jnp.float32
    )
    modulation = lax.psum(mod_terms.reshape(3, dim_local), "seq")
    local_rows = jnp.concatenate([text_tokens[0], image_tokens], axis=1)
    hidden = local_rows.astype(jnp.float32)
    totals, squares = lax.psum(
        (jnp.sum(hidden, axis=-1), jnp.sum(hidden * hidden, axis=-1)), "wblk"
    )
    average = (totals / D)[..., None]
    variance = (squares / D)[..., None] - average * average
    normed = (
        (hidden - average) * lax.rsqrt(variance + epsilon) * (1.0 + modulation[1]) + modulation[0]
    ).astype(jnp.bfloat16)
    gathered = lax.all_gather(normed, "wblk", axis=2, tiled=True)
    token_rows = gathered.reshape(row_count, D)
    projected, mlp_units = input_folder(
        token_rows,
        (
            lax.all_gather(qkv_weight, "seq", axis=0, tiled=True),
            lax.all_gather(up_weight, "seq", axis=0, tiled=True),
        ),
    )
    projected = projected.reshape(prompts, local_len, 3, heads_local, HD)
    image_index = seq_pos * image_rows + jnp.arange(image_rows, dtype=jnp.int32)
    height_pos = jnp.concatenate(
        [jnp.zeros((text_rows,), jnp.float32), (image_index // GRID).astype(jnp.float32)]
    )
    width_pos = jnp.concatenate(
        [jnp.zeros((text_rows,), jnp.float32), (image_index % GRID).astype(jnp.float32)]
    )
    angles = rotary_angles(height_pos, width_pos)
    queries = rotate(head_norm(projected[:, :, 0], query_gain), angles).astype(jnp.bfloat16)
    key_rows = rotate(head_norm(projected[:, :, 1], key_gain), angles).astype(jnp.bfloat16)
    values = projected[:, :, 2].astype(jnp.bfloat16)
    scale_factor = HD ** (-0.5)
    seq_count = lax.psum(1, "seq")
    pair_count = prompts * heads_local
    subs = seq_count // pair_count
    sub_rows = local_len // subs
    pair_keys = key_rows.transpose(0, 2, 1, 3).reshape(pair_count, local_len, HD)
    pair_values = values.transpose(0, 2, 1, 3).reshape(pair_count, local_len, HD)
    pair_queries = queries.transpose(0, 2, 1, 3).reshape(seq_count, sub_rows, HD)
    send = jnp.concatenate(
        [
            jnp.broadcast_to(pair_keys[:, None], (pair_count, subs, local_len, HD)).reshape(
                seq_count, local_len, HD
            ),
            jnp.broadcast_to(pair_values[:, None], (pair_count, subs, local_len, HD)).reshape(
                seq_count, local_len, HD
            ),
            pair_queries,
        ],
        axis=1,
    )
    received = lax.all_to_all(send, "seq", 0, 0, tiled=True)
    key_piece = received[:, :local_len].reshape(seq_count * local_len, HD)
    value_piece = received[:, local_len : 2 * local_len].reshape(seq_count * local_len, HD)
    query_piece = received[:, 2 * local_len :].reshape(seq_count * sub_rows, HD)
    my_prompt = seq_pos // subs // heads_local
    width_keys = key_piece.shape[0]
    where_global = jnp.arange(width_keys, dtype=jnp.int32)
    shard_index = where_global // local_len
    within = where_global % local_len
    text_index = shard_index * text_rows + within
    key_live = (within >= text_rows) | (text_index < lengths[my_prompt])
    scores = jnp.dot(query_piece, key_piece.T, preferred_element_type=jnp.float32) * scale_factor
    scores = jnp.where(key_live[None, :], scores, -1e30)
    top_score = jnp.max(scores, axis=-1, keepdims=True)
    weights = jnp.exp(scores - top_score)
    denominator = jnp.sum(weights, axis=-1, keepdims=True)
    numerator = jnp.dot(
        weights.astype(jnp.bfloat16), value_piece, preferred_element_type=jnp.float32
    )
    mixed = (numerator / denominator).astype(jnp.bfloat16).reshape(seq_count, sub_rows, HD)
    returned = lax.all_to_all(mixed, "seq", 0, 0, tiled=True)
    attended = returned.reshape(prompts, heads_local, local_len, HD)
    attended = attended.transpose(0, 2, 1, 3).reshape(row_count, heads_local * HD)
    activated = jax.nn.gelu(mlp_units, approximate=True).astype(jnp.bfloat16)
    branch_terms = output_folder(
        attended,
        activated,
        (
            lax.all_gather(attn_weight, "seq", axis=1, tiled=True),
            lax.all_gather(down_weight, "seq", axis=1, tiled=True),
        ),
    )
    branch = lax.psum_scatter(
        branch_terms.reshape(prompts, local_len, D).astype(jnp.bfloat16),
        "wblk",
        scatter_dimension=2,
        tiled=True,
    ).astype(jnp.float32)
    layer_out = hidden + modulation[2] * branch
    text_out = layer_out[:, :text_rows].astype(jnp.bfloat16)[None]
    image_out = layer_out[:, text_rows:]
    paired = lax.all_to_all(
        image_out[:, None].astype(jnp.bfloat16), "cfg", split_axis=0, concat_axis=1, tiled=True
    ).astype(jnp.float32)
    velocity = paired[:, 1] + guidance * (paired[:, 0] - paired[:, 1])
    own_prompts = prompts // 2
    latent = lax.dynamic_slice_in_dim(image_tokens, cfg_pos * own_prompts, own_prompts, 0).astype(
        jnp.float32
    )
    new_image = latent + step_size * velocity
    return (text_out, velocity, new_image)


def solution(mesh):
    in_specs = (
        P("cfg", None, "seq", "wblk"),
        P(None, "seq", "wblk"),
        P("cfg", "seq"),
        P("seq", None, "wblk"),
        P("seq", None, "wblk", None),
        P("seq", "wblk"),
        P(),
        P(),
        P("wblk", "seq"),
        P("wblk", "seq"),
        P(),
        P(),
    )
    out_specs = (P("cfg", None, "seq", "wblk"), P("cfg", "seq", "wblk"), P("cfg", "seq", "wblk"))
    return jax.shard_map(shards, mesh=mesh, in_specs=in_specs, out_specs=out_specs, check_vma=False)
```

profile of v0, /device:TPU:2, one launch (start us, length us, event | category | flops | bytes accessed | tf_op | source)
XLA Modules:
  0.0 486.1 jit_solution(3172526040136737661)
XLA Ops:
  8.7 0.8 fusion.63
  9.7 1.3 convert_reduce_fusion
  11.0 15.1 %all-reduce.2 = (f32[2,288]{1,0:T(2,128)S(1)}, f32[2,288]{1,0:T(2,128)S(1)}) all-reduce(f32[2,288]{1,0:T(2,128)S(1)} %get-tuple-element.6, f32[2,288]{1,0:T(2,128)S(1)} %get-tuple-element.5), channel_id=1, replica_groups=mesh['cfg'=2,'seq'=16,'wblk'=8] {'wblk'}, use_global_device_ids=true, to_apply=%region_4.5 | all-reduce | flops 1152 | bytes 9216 | tf_op jit(solution)/shard_map/psum | solution.py:122
  26.1 46.3 %psum.21 = f32[3,384]{1,0:T(4,128)S(1)} all-reduce(f32[3,384]{1,0:T(4,128)S(1)} %bitcast.121), channel_id=1, replica_groups=mesh['cfg'=2,'seq'=16,'wblk'=8] {'seq'}, use_global_device_ids=true, to_apply=%region_0.1 | all-reduce | flops 1152 | bytes 9216 | tf_op jit(solution)/shard_map/psum | solution.py:119
  72.5 2.0 fusion.26
  75.8 0.8 mul.324
  76.6 0.8 mul.305
  78.1 13.8 %all-gather.8.cloned.1.call-done = bf16[3072,3,2,128]{3,2,1,0:T(2,128)(2,1)} async-done(((bf16[192,3,2,128]{3,2,1,0:T(2,128)(2,1)}), bf16[3072,3,2,128]{3,2,1,0:T(2,128)(2,1)}) %all-gather.8.cloned.1.call-update) | async-done | bytes 4718608 | tf_op jit(solution)/shard_map/all_gather | solution.py:135
  91.9 12.4 %copy.38 = bf16[3072,3,2,128]{0,3,2,1:T(8,128)(2,1)} copy(bf16[3072,3,2,128]{3,2,1,0:T(2,128)(2,1)} %all-gather.8.cloned.1.call-done) | data formatting | bytes 9437184 | tf_op jit(solution)/shard_map/reshape | solution.py:77
  104.3 23.6 %all-gather.6.cloned.1.call-done = bf16[2,288,3072]{2,1,0:T(8,128)(2,1)} async-done(((bf16[2,288,384]{2,1,0:T(8,128)(2,1)}), bf16[2,288,3072]{2,1,0:T(8,128)(2,1)}) %all-gather.6.cloned.1.call-update) | async-done | bytes 3538960 | tf_op jit(solution)/shard_map/all_gather | solution.py:130
  127.9 6.8 %fusion.6 = f32[2,288,3,2,128]{4,1,3,2,0:T(8,128)S(1)} fusion(bf16[3072,3,2,128]{0,3,2,1:T(8,128)(2,1)} %copy.38, bf16[2,288,3072]{2,1,0:T(8,128)(2,1)} %all-gather.6.cloned.1.call-done), kind=kOutput, calls=%fused_computation.8 | convolution fusion | flops 2717908992 | bytes 10027008 | tf_op jit(solution)/shard_map/dot_general | solution.py:76
  137.0 0.8 subtract_convert_fusion.1
  140.3 1.7 pad_maximum_fusion
  142.0 10.1 %all-to-all-start = ((bf16[16,648,128]{2,1,0:T(8,128)(2,1)}), bf16[16,648,128]{2,1,0:T(8,128)(2,1)S(1)}, u32[]{:S(2)}, u32[]{:S(2)}) async-start(bf16[16,648,128]{2,1,0:T(8,128)(2,1)} %pad_maximum_fusion), calls=%async_computation | async-start | bytes 5308416 | tf_op jit(solution)/shard_map/all_to_all | solution.py:171
  154.0 100.2 %all-to-all-done = bf16[16,648,128]{2,1,0:T(8,128)(2,1)S(1)} async-done(((bf16[16,648,128]{2,1,0:T(8,128)(2,1)}), bf16[16,648,128]{2,1,0:T(8,128)(2,1)S(1)}, u32[]{:S(2)}, u32[]{:S(2)}) %all-to-all-start) | async-done | bytes 2654240 | tf_op jit(solution)/shard_map/all_to_all | solution.py:171
  254.3 3.5 fusion.70
  257.8 4.2 fusion.1
  262.1 2.8 copy-done.2
  264.9 11.1 %fusion.12 = bf16[1152,128]{1,0:T(8,128)(2,1)} fusion(bf16[4608,128]{1,0:T(8,128)(2,1)S(1)} %bitcast.103, f32[1152,4608]{1,0:T(8,128)} %copy-done.2, f32[1152]{0:T(1024)S(1)} %get-tuple-element.30, f32[1152]{0:T(1024)S(1)} %fusion.1), kind=kOutput, calls=%fused_computation.14 | convolution fusion | flops 1369866240 | bytes 22717440 | tf_op jit(solution)/shard_map/dot_general | solution.py:187
  276.0 6.7 %all-to-all-start.1 = ((bf16[16,72,128]{2,1,0:T(8,128)(2,1)}), bf16[16,72,128]{2,1,0:T(8,128)(2,1)S(1)}, u32[]{:S(2)}, u32[]{:S(2)}) async-start(bf16[16,72,128]{2,1,0:T(8,128)(2,1)} %bitcast.28), calls=%async_computation.1 | async-start | bytes 589824 | tf_op jit(solution)/shard_map/all_to_all | solution.py:191
  283.0 54.5 %all-gather.14.cloned.1.call-done = bf16[768,3072]{0,1:T(8,128)(2,1)} async-done(((bf16[768,192]{0,1:T(8,128)(2,1)}), bf16[768,3072]{0,1:T(8,128)(2,1)}) %all-gather.14.cloned.1.call-update) | async-done | bytes 4718608 | tf_op jit(solution)/shard_map/all_gather | solution.py:200
  337.5 15.0 %fusion.29 = f32[576,3072]{1,0:T(8,128)} fusion(bf16[768,3072]{0,1:T(8,128)(2,1)} %all-gather.14.cloned.1.call-done, bf16[576,3072]{1,0:T(8,128)(2,1)} %bitcast.123, bf16[3072,768]{1,0:T(8,128)(2,1)} %all-gather.12.cloned.1.call-done), kind=kOutput, calls=%fused_computation.33 | convolution fusion | flops 5439799296 | bytes 20054016 | tf_op jit(solution)/shard_map/dot_general | solution.py:85
  352.7 46.0 %all-gather.10.cloned.1.call-done = bf16[256,3072]{0,1:T(8,128)(2,1)} async-done(((bf16[256,192]{0,1:T(8,128)(2,1)}), bf16[256,3072]{0,1:T(8,128)(2,1)}) %all-gather.10.cloned.1.call-update) | async-done | bytes 1572880 | tf_op jit(solution)/shard_map/all_gather | solution.py:199
  398.7 6.5 %add_convert_fusion = bf16[576,3072]{1,0:T(8,128)(2,1)} fusion(f32[576,3072]{1,0:T(8,128)} %fusion.29, bf16[256,3072]{0,1:T(8,128)(2,1)} %all-gather.10.cloned.1.call-done, bf16[72,8,2,128]{3,2,1,0:T(2,128)(2,1)S(1)} %bitcast.113), kind=kOutput, calls=%fused_computation.7 | convolution fusion | flops 909508608 | bytes 12484608 | tf_op jit(solution)/shard_map/dot_general | solution.py:84
  405.2 12.3 %copy.39 = bf16[2,288,3072]{1,0,2:T(2,128)(2,1)} copy(bf16[2,288,3072]{2,1,0:T(8,128)(2,1)} %bitcast.102) | data formatting | bytes 7077888
  417.5 10.2 %reshape.318 = bf16[3072,576]{1,0:T(8,128)(2,1)} reshape(bf16[3072,2,288]{2,1,0:T(2,128)(2,1)} %bitcast.101) | data formatting | bytes 7077888
  427.7 37.4 %reduce-scatter.4.cloned.1.call-done = bf16[384,576]{1,0:T(8,128)(2,1)} async-done(((bf16[3072,576]{1,0:T(8,128)(2,1)}), bf16[384,576]{1,0:T(8,128)(2,1)}) %reduce-scatter.4.cloned.1.call-update) | async-done | bytes 442384
  465.0 2.2 reshape.319
  468.1 0.8 slice_bitcast_fusion.2
  468.9 3.5 all-to-all-start.2
  473.0 5.2 %all-to-all-done.2 = bf16[2,1,256,384]{3,2,1,0:T(8,128)(2,1)S(1)} async-done(((bf16[2,1,256,384]{3,2,1,0:T(8,128)(2,1)}), bf16[2,1,256,384]{3,2,1,0:T(8,128)(2,1)S(1)}, u32[]{:S(2)}, u32[]{:S(2)}) %all-to-all-start.2) | async-done | bytes 393248 | tf_op jit(solution)/shard_map/all_to_all | solution.py:212
  478.3 1.0 multiply_add_fusion
  (62 shorter events, 11.8 us)
Async XLA Ops:
  7.2 2.3 copy-start
  7.2 84.7 %all-gather.8.cloned.1.call-start = ((), (), s32[]{:S(2)}) async-start(), calls=%async_computation.5 | async-start | bytes 5013504 | tf_op jit(solution)/shard_map/all_gather | solution.py:135
  7.9 120.0 %all-gather.6.cloned.1.call-start = ((), (), s32[]{:S(2)}) async-start(), calls=%async_computation.4 | async-start | bytes 3981312 | tf_op jit(solution)/shard_map/all_gather | solution.py:130
  74.5 208.5 %all-gather.12.cloned.1.call-start = ((), (), s32[]{:S(2)}) async-start(), calls=%async_computation.7 | async-start | bytes 5013504 | tf_op jit(solution)/shard_map/all_gather | solution.py:136
  75.2 262.3 %all-gather.14.cloned.1.call-start = ((), (), s32[]{:S(2)}) async-start(), calls=%async_computation.8 | async-start | bytes 5013504 | tf_op jit(solution)/shard_map/all_gather | solution.py:200
  142.0 10.8 %copy-start.5 = (s32[2]{0:T(128)S(1)}, s32[2]{0:T(128)}, u32[]{:S(2)}) copy-start(s32[2]{0:T(128)} %param.22) | copy-start | bytes 28
  142.0 112.2 %all-to-all-start = ((bf16[16,648,128]{2,1,0:T(8,128)(2,1)}), bf16[16,648,128]{2,1,0:T(8,128)(2,1)S(1)}, u32[]{:S(2)}, u32[]{:S(2)}) async-start(bf16[16,648,128]{2,1,0:T(8,128)(2,1)} %pad_maximum_fusion), calls=%async_computation | async-start | bytes 5308416 | tf_op jit(solution)/shard_map/all_to_all | solution.py:171
  152.1 246.6 %all-gather.10.cloned.1.call-start = ((), (), s32[]{:S(2)}) async-start(), calls=%async_computation.6 | async-start | bytes 1671168 | tf_op jit(solution)/shard_map/all_gather | solution.py:199
  257.8 7.1 %copy-start.2 = (f32[1152,4608]{1,0:T(8,128)}, f32[1152,4608]{1,0:T(8,128)S(1)}, u32[]{:S(2)}) copy-start(f32[1152,4608]{1,0:T(8,128)S(1)} %get-tuple-element.31) | copy-start | bytes 63700996
  276.0 76.5 %all-to-all-start.1 = ((bf16[16,72,128]{2,1,0:T(8,128)(2,1)}), bf16[16,72,128]{2,1,0:T(8,128)(2,1)S(1)}, u32[]{:S(2)}, u32[]{:S(2)}) async-start(bf16[16,72,128]{2,1,0:T(8,128)(2,1)} %bitcast.28), calls=%async_computation.1 | async-start | bytes 589824 | tf_op jit(solution)/shard_map/all_to_all | solution.py:191
  282.7 182.3 %reduce-scatter.4.cloned.1.call-start = ((), (), s32[]{:S(2)}) async-start(), calls=%async_computation.9 | async-start | bytes 4423680
  427.6 40.3 %copy-start.3 = (bf16[2,256,384]{2,1,0:T(8,128)(2,1)S(1)}, bf16[2,256,384]{2,1,0:T(8,128)(2,1)}, u32[]{:S(2)}) copy-start(bf16[2,256,384]{2,1,0:T(8,128)(2,1)} %param.13) | copy-start | bytes 1179652
  427.6 40.3 %copy-start.4 = (bf16[1,2,32,384]{3,2,1,0:T(8,128)(2,1)S(1)}, bf16[1,2,32,384]{3,2,1,0:T(8,128)(2,1)}, u32[]{:S(2)}) copy-start(bf16[1,2,32,384]{3,2,1,0:T(8,128)(2,1)} %param.12) | copy-start | bytes 147460
  465.0 14.2 %copy-start.1 = (bf16[192,3,384]{2,0,1:T(8,128)(2,1)S(1)}, bf16[192,3,384]{2,0,1:T(8,128)(2,1)}, u32[]{:S(2)}) copy-start(bf16[192,3,384]{2,0,1:T(8,128)(2,1)} %param.15) | copy-start | bytes 1327108
  468.9 9.3 %all-to-all-start.2 = ((bf16[2,1,256,384]{3,2,1,0:T(8,128)(2,1)}), bf16[2,1,256,384]{3,2,1,0:T(8,128)(2,1)S(1)}, u32[]{:S(2)}, u32[]{:S(2)}) async-start(bf16[2,1,256,384]{3,2,1,0:T(8,128)(2,1)} %slice_bitcast_fusion.2), calls=%async_computation.2 | async-start | bytes 786432 | tf_op jit(solution)/shard_map/all_to_all | solution.py:212
Sparse Core Ops, SparseCore 0:
  10.4 81.3 all-gather.7
  93.7 34.1 all-gather.5
  130.3 120.7 all-gather.11
  253.4 84.1 all-gather.13
  339.8 58.8 all-gather.9
  427.8 37.2 reduce-scatter.3
where the time goes:
time: 488 us; the launch traced here: 486 us
  waiting for transfers between devices  283 us (58%)
  blocking collectives  61.4 us (13%)
  local copies, waits for them, and re-layouts  47.1 us (10%)
  matrix products  43 us (9%)
  starting transfers between devices  20.9 us (4%)
  other arithmetic  15.6 us (3%)
  between operations  15.2 us (3%)
    all_to_all x1, waiting for transfers between devices, shards(): received = lax.all_to_all(send, 'seq', 0, 0, tiled=True)  100 us
    all_gather x1, waiting for transfers between devices, shards(): lax.all_gather(down_weight, 'seq', axis=1, tiled=True)  54.5 us
    psum x1, blocking collectives, shards(): modulation = lax.psum(mod_terms.reshape(3, dim_local), 'seq')  46.3 us
    all_gather x1, waiting for transfers between devices, shards(): lax.all_gather(attn_weight, 'seq', axis=1, tiled=True)  46 us
    unnamed x7, waiting for transfers between devices  39.6 us
    unnamed x16, local copies, waits for them, and re-layouts  28.2 us
    all_gather x1, waiting for transfers between devices, shards(): gathered = lax.all_gather(normed, 'wblk', axis=2, tiled=True)  23.6 us
    psum x1, blocking collectives, shards(): lax.psum((jnp.sum(hidden, axis=-1), jnp.sum(hidden * hidden, axis=-1)), '...  15.1 us
  transfers between devices with their start and end apart: 9, of which 7 were waited for; matrix products, arithmetic and copies ran while one was open for 14% of the time, Pallas kernels for 0%

commit v1 on v0

--- a/solution.py
+++ b/solution.py
@@ -127,7 +127,9 @@
     normed = (
         (hidden - average) * lax.rsqrt(variance + epsilon) * (1.0 + modulation[1]) + modulation[0]
     ).astype(jnp.bfloat16)
-    gathered = lax.all_gather(normed, "wblk", axis=2, tiled=True)
+    gathered = jnp.concatenate(
+        lax.all_to_all(jnp.stack([normed] * lax.axis_size("wblk")), "wblk", 0, 0), axis=2
+    )
     token_rows = gathered.reshape(row_count, D)
     projected, mlp_units = input_folder(
         token_rows,

time: 488 us -> 454 us (0.930)
  waiting for transfers between devices: 283 us -> 227 us
  local copies, waits for them, and re-layouts: 47.1 us -> 65.3 us
  starting transfers between devices: 20.9 us -> 26.4 us
    all_gather x1, waiting for transfers between devices: 54.5 us -> 0.02 us  [shards(): lax.all_gather(down_weight, 'seq', axis=1, tiled=True)]
    all_to_all x0 -> x1, waiting for transfers between devices: none -> 40.9 us  [shards(): lax.all_to_all(jnp.stack([normed] * lax.axis_size('wblk')), 'wblk', 0, 0)]
    all_to_all x1, waiting for transfers between devices: 100 us -> 63.7 us  [shards(): received = lax.all_to_all(send, 'seq', 0, 0, tiled=True)]
    all_gather x1, waiting for transfers between devices: 0.02 us -> 35.3 us  [shards(): lax.all_gather(up_weight, 'seq', axis=0, tiled=True)]
    all_gather x1 -> x0, waiting for transfers between devices: 23.6 us -> none  [shards(): gathered = lax.all_gather(normed, 'wblk', axis=2, tiled=True)]
    all_gather x1, waiting for transfers between devices: 13.8 us -> 0.01 us  [shards(): lax.all_gather(qkv_weight, 'seq', axis=0, tiled=True)]
    dot_general x0 -> x1, local copies, waits for them, and re-layouts: none -> 6.61 us  [input_folder(): jnp.dot(source, pieces[0].reshape(width_rows, -1), preferred_element_type...]
    reshape x0 -> x1, local copies, waits for them, and re-layouts: none -> 5.9 us  [shards(): jnp.concatenate(lax.all_to_all(jnp.stack([normed] * lax.axis_size('wblk')...]
  transfers between devices with their start and end apart: 9 -> 9, of which waited for: 7 -> 6; matrix products, arithmetic and copies ran while one was open for 14% -> 19% of each run, Pallas kernels for 0% -> 0%
where the time goes in v1:
time: 454 us; the launch traced here: 453 us
  waiting for transfers between devices  227 us (50%)
  local copies, waits for them, and re-layouts  65.3 us (14%)
  blocking collectives  60.9 us (13%)
  matrix products  43.2 us (10%)
  starting transfers between devices  26.4 us (6%)
  other arithmetic  14.9 us (3%)
  between operations  14.9 us (3%)
    all_to_all x1, waiting for transfers between devices, shards(): received = lax.all_to_all(send, 'seq', 0, 0, tiled=True)  63.7 us
    psum x1, blocking collectives, shards(): modulation = lax.psum(mod_terms.reshape(3, dim_local), 'seq')  45.8 us
    all_gather x1, waiting for transfers between devices, shards(): lax.all_gather(attn_weight, 'seq', axis=1, tiled=True)  42.3 us
    all_to_all x1, waiting for transfers between devices, shards(): lax.all_to_all(jnp.stack([normed] * lax.axis_size('wblk')), 'wblk', 0, 0)  40.9 us
    unnamed x6, waiting for transfers between devices  39.8 us
    all_gather x1, waiting for transfers between devices, shards(): lax.all_gather(up_weight, 'seq', axis=0, tiled=True)  35.3 us
    unnamed x21, local copies, waits for them, and re-layouts  32.8 us
    psum x1, blocking collectives, shards(): lax.psum((jnp.sum(hidden, axis=-1), jnp.sum(hidden * hidden, axis=-1)), '...  15.1 us
  transfers between devices with their start and end apart: 9, of which 6 were waited for; matrix products, arithmetic and copies ran while one was open for 19% of the time, Pallas kernels for 0%

profile of v1, /device:TPU:2, one launch (start us, length us, event | category | flops | bytes accessed | tf_op | source)
XLA Modules:
  0.0 452.7 jit_solution(3137220092038886451)
XLA Ops:
  10.4 1.3 convert_reduce_fusion
  11.7 15.1 %all-reduce.2 = (f32[2,288]{1,0:T(2,128)S(1)}, f32[2,288]{1,0:T(2,128)S(1)}) all-reduce(f32[2,288]{1,0:T(2,128)S(1)} %get-tuple-element.6, f32[2,288]{1,0:T(2,128)S(1)} %get-tuple-element.5), channel_id=1, replica_groups=mesh['cfg'=2,'seq'=16,'wblk'=8] {'wblk'}, use_global_device_ids=true, to_apply=%region_4.5 | all-reduce | flops 1152 | bytes 9216 | tf_op jit(solution)/shard_map/psum | solution.py:122
  26.8 45.8 %psum.21 = f32[3,384]{1,0:T(4,128)S(1)} all-reduce(f32[3,384]{1,0:T(4,128)S(1)} %bitcast.126), channel_id=1, replica_groups=mesh['cfg'=2,'seq'=16,'wblk'=8] {'seq'}, use_global_device_ids=true, to_apply=%region_0.1 | all-reduce | flops 1152 | bytes 9216 | tf_op jit(solution)/shard_map/psum | solution.py:119
  72.7 1.3 fusion.26
  74.0 2.2 stack.8
  76.2 4.6 %all-to-all-start = ((bf16[8,2,288,384]{3,2,1,0:T(8,128)(2,1)}), bf16[8,2,288,384]{3,2,1,0:T(8,128)(2,1)}, u32[]{:S(2)}, u32[]{:S(2)}) async-start(bf16[8,2,288,384]{3,2,1,0:T(8,128)(2,1)} %stack.8), calls=%async_computation | async-start | bytes 7077888 | tf_op jit(solution)/shard_map/all_to_all | solution.py:131
  82.6 40.9 %all-to-all-done = bf16[8,2,288,384]{3,2,1,0:T(8,128)(2,1)} async-done(((bf16[8,2,288,384]{3,2,1,0:T(8,128)(2,1)}), bf16[8,2,288,384]{3,2,1,0:T(8,128)(2,1)}, u32[]{:S(2)}, u32[]{:S(2)}) %all-to-all-start) | async-done | bytes 3538976 | tf_op jit(solution)/shard_map/all_to_all | solution.py:131
  123.5 5.9 %copy.37 = bf16[2,288,8,384]{3,2,1,0:T(8,128)(2,1)} copy(bf16[2,288,8,384]{3,1,0,2:T(8,128)(2,1)} %bitcast.6) | data formatting | bytes 7077888 | tf_op jit(solution)/shard_map/reshape | solution.py:130
  129.4 6.6 %reshape.324 = bf16[2,288,3072,1,1]{2,1,0,3,4:T(8,128)(2,1)} reshape(bf16[2,288,8,384]{3,2,1,0:T(8,128)(2,1)} %copy.37) | data formatting | bytes 7077888 | tf_op jit(solution)/shard_map/dot_general | solution.py:76
  136.0 12.6 %copy.49 = bf16[3072,3,2,128]{0,3,2,1:T(8,128)(2,1)} copy(bf16[3072,3,2,128]{3,2,1,0:T(2,128)(2,1)} %all-gather.5.cloned.1.call-done) | data formatting | bytes 9437184 | tf_op jit(solution)/shard_map/reshape | solution.py:77
  148.6 6.9 %fusion.6 = f32[2,288,3,2,128]{4,1,3,2,0:T(8,128)S(1)} fusion(bf16[3072,3,2,128]{0,3,2,1:T(8,128)(2,1)} %copy.49, bf16[2,288,3072,1,1]{2,1,0,3,4:T(8,128)(2,1)} %reshape.324), kind=kOutput, calls=%fused_computation.8 | convolution fusion | flops 2717908992 | bytes 10027008 | tf_op jit(solution)/shard_map/dot_general | solution.py:76
  157.8 0.8 subtract_convert_fusion.1
  161.1 1.7 pad_maximum_fusion
  162.7 9.3 %all-to-all-start.1 = ((bf16[16,648,128]{2,1,0:T(8,128)(2,1)}), bf16[16,648,128]{2,1,0:T(8,128)(2,1)S(1)}, u32[]{:S(2)}, u32[]{:S(2)}) async-start(bf16[16,648,128]{2,1,0:T(8,128)(2,1)} %pad_maximum_fusion), calls=%async_computation.1 | async-start | bytes 5308416 | tf_op jit(solution)/shard_map/all_to_all | solution.py:173
  173.9 4.6 %copy.55 = bf16[72,8,8,384]{3,1,2,0:T(8,128)(2,1)} copy(bf16[72,8,8,384]{3,2,1,0:T(8,128)(2,1)} %bitcast.104) | data formatting | bytes 7077888
  178.6 63.7 %all-to-all-done.1 = bf16[16,648,128]{2,1,0:T(8,128)(2,1)S(1)} async-done(((bf16[16,648,128]{2,1,0:T(8,128)(2,1)}), bf16[16,648,128]{2,1,0:T(8,128)(2,1)S(1)}, u32[]{:S(2)}, u32[]{:S(2)}) %all-to-all-start.1) | async-done | bytes 2654240 | tf_op jit(solution)/shard_map/all_to_all | solution.py:173
  242.4 3.5 fusion.70
  245.9 4.2 fusion.1
  250.2 2.8 copy-done.2
  253.0 11.2 %fusion.12 = bf16[1152,128]{1,0:T(8,128)(2,1)} fusion(bf16[4608,128]{1,0:T(8,128)(2,1)S(1)} %bitcast.107, f32[1152,4608]{1,0:T(8,128)} %copy-done.2, f32[1152]{0:T(1024)S(1)} %get-tuple-element.30, f32[1152]{0:T(1024)S(1)} %fusion.1), kind=kOutput, calls=%fused_computation.14 | convolution fusion | flops 1369866240 | bytes 22717440 | tf_op jit(solution)/shard_map/dot_general | solution.py:189
  264.2 8.3 %all-to-all-start.2 = ((bf16[16,72,128]{2,1,0:T(8,128)(2,1)}), bf16[16,72,128]{2,1,0:T(8,128)(2,1)S(1)}, u32[]{:S(2)}, u32[]{:S(2)}) async-start(bf16[16,72,128]{2,1,0:T(8,128)(2,1)} %bitcast.28), calls=%async_computation.2 | async-start | bytes 589824 | tf_op jit(solution)/shard_map/all_to_all | solution.py:193
  272.8 35.3 %all-gather.9.cloned.1.call-done = bf16[3072,768]{1,0:T(8,128)(2,1)} async-done(((bf16[192,768]{1,0:T(8,128)(2,1)}), bf16[3072,768]{1,0:T(8,128)(2,1)}) %all-gather.9.cloned.1.call-update) | async-done | bytes 4718608 | tf_op jit(solution)/shard_map/all_gather | solution.py:138
  308.1 15.0 %fusion.29 = f32[576,3072]{1,0:T(8,128)} fusion(bf16[768,3072]{0,1:T(8,128)(2,1)} %all-gather.11.cloned.1.call-done, bf16[576,3072]{1,0:T(8,128)(2,1)} %bitcast.111, bf16[3072,768]{1,0:T(8,128)(2,1)} %all-gather.9.cloned.1.call-done), kind=kOutput, calls=%fused_computation.33 | convolution fusion | flops 5439799296 | bytes 20054016 | tf_op jit(solution)/shard_map/dot_general | solution.py:85
  323.4 42.3 %all-gather.7.cloned.1.call-done = bf16[256,3072]{0,1:T(8,128)(2,1)} async-done(((bf16[256,192]{0,1:T(8,128)(2,1)}), bf16[256,3072]{0,1:T(8,128)(2,1)}) %all-gather.7.cloned.1.call-update) | async-done | bytes 1572880 | tf_op jit(solution)/shard_map/all_gather | solution.py:201
  365.7 6.5 %add_convert_fusion = bf16[576,3072]{1,0:T(8,128)(2,1)} fusion(f32[576,3072]{1,0:T(8,128)} %fusion.29, bf16[256,3072]{0,1:T(8,128)(2,1)} %all-gather.7.cloned.1.call-done, bf16[72,8,2,128]{3,2,1,0:T(2,128)(2,1)S(1)} %bitcast.118), kind=kOutput, calls=%fused_computation.7 | convolution fusion | flops 909508608 | bytes 12484608 | tf_op jit(solution)/shard_map/dot_general | solution.py:84
  372.2 12.3 %copy.50 = bf16[2,288,3072]{1,0,2:T(2,128)(2,1)} copy(bf16[2,288,3072]{2,1,0:T(8,128)(2,1)} %bitcast.106) | data formatting | bytes 7077888
  384.4 10.2 %reshape.327 = bf16[3072,576]{1,0:T(8,128)(2,1)} reshape(bf16[3072,2,288]{2,1,0:T(2,128)(2,1)} %bitcast.105) | data formatting | bytes 7077888
  394.6 37.4 %reduce-scatter.4.cloned.1.call-done = bf16[384,576]{1,0:T(8,128)(2,1)} async-done(((bf16[3072,576]{1,0:T(8,128)(2,1)}), bf16[384,576]{1,0:T(8,128)(2,1)}) %reduce-scatter.4.cloned.1.call-update) | async-done | bytes 442384
  432.0 2.2 reshape.328
  435.9 3.5 all-to-all-start.3
  440.0 5.2 %all-to-all-done.3 = bf16[2,1,256,384]{3,2,1,0:T(8,128)(2,1)S(1)} async-done(((bf16[2,1,256,384]{3,2,1,0:T(8,128)(2,1)}), bf16[2,1,256,384]{3,2,1,0:T(8,128)(2,1)S(1)}, u32[]{:S(2)}, u32[]{:S(2)}) %all-to-all-start.3) | async-done | bytes 393248 | tf_op jit(solution)/shard_map/all_to_all | solution.py:214
  445.2 1.0 multiply_add_fusion
  (69 shorter events, 13.8 us)
Async XLA Ops:
  7.2 3.1 copy-start
  7.2 128.8 %all-gather.5.cloned.1.call-start = ((), (), s32[]{:S(2)}) async-start(), calls=%async_computation.5 | async-start | bytes 5013504 | tf_op jit(solution)/shard_map/all_gather | solution.py:137
  7.9 264.9 %all-gather.11.cloned.1.call-start = ((), (), s32[]{:S(2)}) async-start(), calls=%async_computation.8 | async-start | bytes 5013504 | tf_op jit(solution)/shard_map/all_gather | solution.py:202
  76.2 5.4 %copy-start.5 = (f32[128]{0:T(128)S(1)}, f32[128]{0:T(128)}, u32[]{:S(2)}) copy-start(f32[128]{0:T(128)} %param.18) | copy-start | bytes 1540
  76.2 5.5 %copy-start.6 = (f32[128]{0:T(128)S(1)}, f32[128]{0:T(128)}, u32[]{:S(2)}) copy-start(f32[128]{0:T(128)} %param.19) | copy-start | bytes 1540
  76.2 47.3 %all-to-all-start = ((bf16[8,2,288,384]{3,2,1,0:T(8,128)(2,1)}), bf16[8,2,288,384]{3,2,1,0:T(8,128)(2,1)}, u32[]{:S(2)}, u32[]{:S(2)}) async-start(bf16[8,2,288,384]{3,2,1,0:T(8,128)(2,1)} %stack.8), calls=%async_computation | async-start | bytes 7077888 | tf_op jit(solution)/shard_map/all_to_all | solution.py:131
  80.9 227.3 %all-gather.9.cloned.1.call-start = ((), (), s32[]{:S(2)}) async-start(), calls=%async_computation.7 | async-start | bytes 5013504 | tf_op jit(solution)/shard_map/all_gather | solution.py:138
  162.7 9.9 %copy-start.7 = (s32[2]{0:T(128)S(1)}, s32[2]{0:T(128)}, u32[]{:S(2)}) copy-start(s32[2]{0:T(128)} %param.22) | copy-start | bytes 28
  162.7 79.5 %all-to-all-start.1 = ((bf16[16,648,128]{2,1,0:T(8,128)(2,1)}), bf16[16,648,128]{2,1,0:T(8,128)(2,1)S(1)}, u32[]{:S(2)}, u32[]{:S(2)}) async-start(bf16[16,648,128]{2,1,0:T(8,128)(2,1)} %pad_maximum_fusion), calls=%async_computation.1 | async-start | bytes 5308416 | tf_op jit(solution)/shard_map/all_to_all | solution.py:173
  172.0 193.7 %all-gather.7.cloned.1.call-start = ((), (), s32[]{:S(2)}) async-start(), calls=%async_computation.6 | async-start | bytes 1671168 | tf_op jit(solution)/shard_map/all_gather | solution.py:201
  245.9 7.1 %copy-start.2 = (f32[1152,4608]{1,0:T(8,128)}, f32[1152,4608]{1,0:T(8,128)S(1)}, u32[]{:S(2)}) copy-start(f32[1152,4608]{1,0:T(8,128)S(1)} %get-tuple-element.31) | copy-start | bytes 63700996
  264.2 59.0 %all-to-all-start.2 = ((bf16[16,72,128]{2,1,0:T(8,128)(2,1)}), bf16[16,72,128]{2,1,0:T(8,128)(2,1)S(1)}, u32[]{:S(2)}, u32[]{:S(2)}) async-start(bf16[16,72,128]{2,1,0:T(8,128)(2,1)} %bitcast.28), calls=%async_computation.2 | async-start | bytes 589824 | tf_op jit(solution)/shard_map/all_to_all | solution.py:193
  272.5 159.5 %reduce-scatter.4.cloned.1.call-start = ((), (), s32[]{:S(2)}) async-start(), calls=%async_computation.9 | async-start | bytes 4423680
  394.6 40.3 %copy-start.3 = (bf16[2,256,384]{2,1,0:T(8,128)(2,1)S(1)}, bf16[2,256,384]{2,1,0:T(8,128)(2,1)}, u32[]{:S(2)}) copy-start(bf16[2,256,384]{2,1,0:T(8,128)(2,1)} %param.13) | copy-start | bytes 1179652
  394.6 40.3 %copy-start.4 = (bf16[1,2,32,384]{3,2,1,0:T(8,128)(2,1)S(1)}, bf16[1,2,32,384]{3,2,1,0:T(8,128)(2,1)}, u32[]{:S(2)}) copy-start(bf16[1,2,32,384]{3,2,1,0:T(8,128)(2,1)} %param.12) | copy-start | bytes 147460
  432.0 14.2 %copy-start.1 = (bf16[192,3,384]{2,0,1:T(8,128)(2,1)S(1)}, bf16[192,3,384]{2,0,1:T(8,128)(2,1)}, u32[]{:S(2)}) copy-start(bf16[192,3,384]{2,0,1:T(8,128)(2,1)} %param.15) | copy-start | bytes 1327108
  435.9 9.3 %all-to-all-start.3 = ((bf16[2,1,256,384]{3,2,1,0:T(8,128)(2,1)}), bf16[2,1,256,384]{3,2,1,0:T(8,128)(2,1)S(1)}, u32[]{:S(2)}, u32[]{:S(2)}) async-start(bf16[2,1,256,384]{3,2,1,0:T(8,128)(2,1)} %slice_bitcast_fusion.2), calls=%async_computation.3 | async-start | bytes 786432 | tf_op jit(solution)/shard_map/all_to_all | solution.py:214
Sparse Core Ops, SparseCore 0:
  10.4 81.7 all-gather.4
  94.6 80.2 all-gather.10
  177.4 130.7 all-gather.8
  310.4 55.2 all-gather.6
  394.7 37.2 reduce-scatter.3
